TPU v7x, 32 devices: a whole 2x2x4 slice. The times are simulated.
32 devices in a mesh: blk: 8 (over z, core), vb: 4 (over y, x).
Axes of the slice: x: 2, y: 2, z: 4, core: 2. Of those that a mesh axis runs over, the one named last changes fastest.
Arguments:
- amplitudes: float32 [32, 1024, 1024], P('blk', 'vb'), may hold values from -6 to 6
- integrals: float32 [2048, 1024], P('blk'), may hold values from -0.5 to 0.5
- row_orbitals: int32 [2048], P('blk'), may hold values from 0 to 1023
- pair_orbitals: int32 [32, 2], P('blk'), may hold values from 0 to 255
- occupied_energy: float32 [256], replicated, may hold values from -2 to -0.5
- virtual_energy: float32 [1024], replicated, may hold values from 0.5 to 3
Outputs:
- density: float32 [32, 1024, 1024], P('blk', 'vb')
All inputs are finite; a program needn't handle non-finite values.
Results may differ from a plain program's by a relative error of at most 0.0003.
Values sent between devices are 32-bit elements; how exact they have to be, the bound alone decides.
No kernel may reach another device: no remote copies, remote signals or barrier semaphores. Data moves between devices by JAX's collectives and lax.ppermute only.
A program may use at most 64 MiB of HBM per device.

v0:
```python
import jax
import jax.numpy as jnp
from jax import lax
from jax.sharding import PartitionSpec as P

HOPS = 5


def passed_along(block, axis, distance):
    devices = range(lax.axis_size(axis))
    route = [((i - distance) % len(devices), i) for i in devices]
    return lax.ppermute(block, axis, route)


def step_down(carried):
    return passed_along(carried, "blk", 1)


def local(amplitudes, integrals, row_orbitals, pair_orbitals, occupied_energy, virtual_energy):
    width = virtual_energy.shape[0]
    nocc = occupied_energy.shape[0]
    quarter = width // lax.axis_size("vb")
    qstart = lax.axis_index("vb") * quarter
    virt_iota = jnp.arange(width, dtype=jnp.int32)
    occ_iota = jnp.arange(nocc, dtype=jnp.int32)
    row_energy = jnp.sum(
        jnp.where(row_orbitals[:, None] == virt_iota[None, :], virtual_energy[None, :], 0.0), axis=1
    )
    pair_match = pair_orbitals[:, :, None] == occ_iota[None, None, :]
    pair_energy = jnp.sum(jnp.where(pair_match, occupied_energy[None, None, :], 0.0), axis=(1, 2))
    own_virtual = lax.dynamic_slice_in_dim(virtual_energy, qstart, quarter, 0)
    own = (integrals, row_energy)
    window = [own]
    current = passed_along((own[0], own[1]), "blk", -(HOPS - HOPS // 2))
    window = [current]
    for turn in range(HOPS):
        current = step_down(current)
        window.append(current)
    factors = lax.all_to_all(amplitudes, "vb", split_axis=2, concat_axis=1, tiled=True)

    def pair_columns(inputs):
        factor, energy = inputs
        total = jnp.zeros((width, quarter), jnp.float32)
        for block, energies in window:
            denom = energies[:, None] + own_virtual[None, :] - energy
            weighted = jnp.dot(
                block, factor, precision=lax.Precision.HIGHEST, preferred_element_type=jnp.float32
            )
            total = total + jnp.dot(
                block.T,
                weighted / denom,
                precision=lax.Precision.HIGHEST,
                preferred_element_type=jnp.float32,
            )
        return total

    totals = lax.map(pair_columns, (factors, pair_energy))
    return lax.all_to_all(totals, "vb", split_axis=1, concat_axis=2, tiled=True)


def solution(mesh):
    return jax.shard_map(
        local,
        mesh=mesh,
        in_specs=(P("blk", "vb", None), P("blk", None), P("blk"), P("blk", None), P(), P()),
        out_specs=P("blk", "vb", None),
        check_vma=False,
    )
```

profile of v0, /device:TPU:0, one launch (start us, length us, event | category | flops | bytes accessed | tf_op | source)
XLA Modules:
  0.0 425.2 jit_solution(7205439664500854542)
XLA Ops:
  3.5 22.9 %collective-permute-done = f32[256,1024]{1,0:T(8,128)S(1)} collective-permute-done((f32[256,1024]{1,0:T(8,128)}, f32[256,1024]{1,0:T(8,128)S(1)}, u32[]{:S(2)}, u32[]{:S(2)}) %collective-permute-start) | collective-permute-done | bytes 1048608 | tf_op jit(solution)/shard_map/ppermute | solution.py:12
  26.4 12.8 %collective-permute-start.2 = (f32[256,1024]{1,0:T(8,128)S(1)}, f32[256,1024]{1,0:T(8,128)S(1)}, u32[]{:S(2)}, u32[]{:S(2)}) collective-permute-start(f32[256,1024]{1,0:T(8,128)S(1)} %collective-permute-done), channel_id=1, source_target_pairs={{28,0},{0,4},{4,8},{8,12},{12,16},{16,20},{20,24},{24,28},{29,1},{... | collective-permute-start | bytes 3145736 | tf_op jit(solution)/shard_map/ppermute | solution.py:12
  39.2 15.6 %collective-permute-done.2 = f32[256,1024]{1,0:T(8,128)S(1)} collective-permute-done((f32[256,1024]{1,0:T(8,128)S(1)}, f32[256,1024]{1,0:T(8,128)S(1)}, u32[]{:S(2)}, u32[]{:S(2)}) %collective-permute-start.2) | collective-permute-done | bytes 1048608 | tf_op jit(solution)/shard_map/ppermute | solution.py:12
  54.8 5.3 %copy.15 = f32[4,256,1024]{1,0,2:T(4,128)} copy(f32[4,256,1024]{2,1,0:T(8,128)} %param.8) | data formatting | bytes 8388608 | tf_op args[0]
  60.1 5.0 %all-to-all-start = ((f32[4,256,1024]{1,0,2:T(4,128)}), f32[4,256,1024]{1,0,2:T(4,128)}, u32[]{:S(2)}, u32[]{:S(2)}) async-start(f32[4,256,1024]{1,0,2:T(4,128)} %copy.15), calls=%async_computation | async-start | bytes 8388608 | tf_op jit(solution)/shard_map/all_to_all | solution.py:39
  65.1 5.7 %collective-permute-done.4 = f32[256,1024]{1,0:T(8,128)S(1)} collective-permute-done((f32[256,1024]{1,0:T(8,128)S(1)}, f32[256,1024]{1,0:T(8,128)S(1)}, u32[]{:S(2)}, u32[]{:S(2)}) %collective-permute-start.4) | collective-permute-done | bytes 1048608 | tf_op jit(solution)/shard_map/ppermute | solution.py:12
  70.8 16.0 %collective-permute-done.6 = f32[256,1024]{1,0:T(8,128)S(1)} collective-permute-done((f32[256,1024]{1,0:T(8,128)S(1)}, f32[256,1024]{1,0:T(8,128)S(1)}, u32[]{:S(2)}, u32[]{:S(2)}) %collective-permute-start.6) | collective-permute-done | bytes 1048608 | tf_op jit(solution)/shard_map/ppermute | solution.py:12
  87.9 16.1 %collective-permute-done.8 = f32[256,1024]{1,0:T(8,128)} collective-permute-done((f32[256,1024]{1,0:T(8,128)S(1)}, f32[256,1024]{1,0:T(8,128)}, u32[]{:S(2)}, u32[]{:S(2)}) %collective-permute-start.8) | collective-permute-done | bytes 1048608 | tf_op jit(solution)/shard_map/ppermute | solution.py:12
  110.3 10.6 %collective-permute-done.3 = f32[256]{0:T(256)S(1)} collective-permute-done((f32[256]{0:T(256)S(1)}, f32[256]{0:T(256)S(1)}, u32[]{:S(2)}, u32[]{:S(2)}) %collective-permute-start.3) | collective-permute-done | bytes 1056 | tf_op jit(solution)/shard_map/ppermute | solution.py:12
  120.9 4.8 %collective-permute-done.5 = f32[256]{0:T(256)S(1)} collective-permute-done((f32[256]{0:T(256)S(1)}, f32[256]{0:T(256)S(1)}, u32[]{:S(2)}, u32[]{:S(2)}) %collective-permute-start.5) | collective-permute-done | bytes 1056 | tf_op jit(solution)/shard_map/ppermute | solution.py:12
  125.7 4.8 %collective-permute-done.7 = f32[256]{0:T(256)S(1)} collective-permute-done((f32[256]{0:T(256)S(1)}, f32[256]{0:T(256)S(1)}, u32[]{:S(2)}, u32[]{:S(2)}) %collective-permute-start.7) | collective-permute-done | bytes 1056 | tf_op jit(solution)/shard_map/ppermute | solution.py:12
  130.5 4.8 %collective-permute-done.9 = f32[256]{0:T(256)S(1)} collective-permute-done((f32[256]{0:T(256)S(1)}, f32[256]{0:T(256)S(1)}, u32[]{:S(2)}, u32[]{:S(2)}) %collective-permute-start.9) | collective-permute-done | bytes 1056 | tf_op jit(solution)/shard_map/ppermute | solution.py:12
  135.6 5.2 %copy.16 = f32[4,4,256,256]{3,2,1,0:T(8,128)} copy(f32[4,4,256,256]{2,0,3,1:T(4,128)} %bitcast.11) | data formatting | bytes 8388608 | tf_op jit(solution)/shard_map/all_to_all | solution.py:39
  140.8 225.5 %while.10 = (s32[]{:T(128)}, f32[4,1024,256]{2,0,1:T(4,128)}, f32[4,1024,256]{2,1,0:T(8,128)}, f32[256,1024]{1,0:T(8,128)S(1)}, f32[256]{0:T(256)S(1)}, /*index=...) while((s32[]{:T(128)}, f32[4,1024,256]{2,0,1:T(4,128)}, ...), condition=%wide.region_3.4_spmd, body=%wide.region_2.3_spmd.sunk | while | flops 9666166784 | bytes 58733852 | solution.py:57
  141.7 4.1 fusion.100
  157.5 3.7 fusion.105
  163.5 3.7 fusion.106
  174.1 23.2 %dynamic_update_slice.5 = f32[4,1024,256]{2,0,1:T(4,128)} dynamic-update-slice(f32[4,1024,256]{2,0,1:T(4,128)} %get-tuple-element.250, f32[1,1024,256]{2,0,1:T(1,128)} %copy.24, s32[]{:T(128)} %get-tuple-element.249, s32[]{:T(128)} %constant.3.clone.1..sunk, s32[]{:T(128)} %constant.3.clone.1..sunk) | dynamic-update-slice | bytes 2097156 | tf_op jit(solution)/shard_map/while/body/jit(dynamic_update_index_in_dim)/dynamic_update_slice | solution.py:57
  198.0 4.1 fusion.100
  213.9 3.7 fusion.105
  219.9 3.7 fusion.106
  230.5 23.2 %dynamic_update_slice.5 = f32[4,1024,256]{2,0,1:T(4,128)} dynamic-update-slice(f32[4,1024,256]{2,0,1:T(4,128)} %get-tuple-element.250, f32[1,1024,256]{2,0,1:T(1,128)} %copy.24, s32[]{:T(128)} %get-tuple-element.249, s32[]{:T(128)} %constant.3.clone.1..sunk, s32[]{:T(128)} %constant.3.clone.1..sunk) | dynamic-update-slice | bytes 2097156 | tf_op jit(solution)/shard_map/while/body/jit(dynamic_update_index_in_dim)/dynamic_update_slice | solution.py:57
  254.4 4.1 fusion.100
  270.2 3.7 fusion.105
  276.2 3.7 fusion.106
  286.8 23.2 %dynamic_update_slice.5 = f32[4,1024,256]{2,0,1:T(4,128)} dynamic-update-slice(f32[4,1024,256]{2,0,1:T(4,128)} %get-tuple-element.250, f32[1,1024,256]{2,0,1:T(1,128)} %copy.24, s32[]{:T(128)} %get-tuple-element.249, s32[]{:T(128)} %constant.3.clone.1..sunk, s32[]{:T(128)} %constant.3.clone.1..sunk) | dynamic-update-slice | bytes 2097156 | tf_op jit(solution)/shard_map/while/body/jit(dynamic_update_index_in_dim)/dynamic_update_slice | solution.py:57
  310.7 4.1 fusion.100
  326.5 3.7 fusion.105
  343.1 23.2 %dynamic_update_slice.5 = f32[4,1024,256]{2,0,1:T(4,128)} dynamic-update-slice(f32[4,1024,256]{2,0,1:T(4,128)} %get-tuple-element.250, f32[1,1024,256]{2,0,1:T(1,128)} %copy.24, s32[]{:T(128)} %get-tuple-element.249, s32[]{:T(128)} %constant.3.clone.1..sunk, s32[]{:T(128)} %constant.3.clone.1..sunk) | dynamic-update-slice | bytes 2097156 | tf_op jit(solution)/shard_map/while/body/jit(dynamic_update_index_in_dim)/dynamic_update_slice | solution.py:57
  366.4 48.4 %all_to_all.36 = f32[4,1024,256]{2,0,1:T(4,128)S(1)} all-to-all(f32[4,1024,256]{2,0,1:T(4,128)} %get-tuple-element.92), channel_id=1, replica_groups=mesh['blk'=8,'vb'=4] {'vb'}, dimensions={1} | all-to-all | bytes 8388608 | tf_op jit(solution)/shard_map/all_to_all | solution.py:58
  414.8 4.7 %copy.18 = f32[4,256,4,256]{3,2,1,0:T(4,128)} copy(f32[4,256,4,256]{3,0,1,2:T(4,128)S(1)} %bitcast.132) | data formatting | bytes 8388608 | tf_op jit(solution)/shard_map/all_to_all | solution.py:58
  419.5 5.8 %all_to_all.33 = f32[4,256,1024]{2,1,0:T(8,128)} reshape(f32[4,256,4,256]{3,2,1,0:T(4,128)} %copy.18) | data formatting | bytes 8388608 | tf_op jit(solution)/shard_map/all_to_all | solution.py:58
  (90 shorter events, 100.7 us)
Async XLA Ops:
  0.0 26.4 %collective-permute-start = (f32[256,1024]{1,0:T(8,128)}, f32[256,1024]{1,0:T(8,128)S(1)}, u32[]{:S(2)}, u32[]{:S(2)}) collective-permute-start(f32[256,1024]{1,0:T(8,128)} %param.9), channel_id=1, source_target_pairs={{12,0},{16,4},{20,8},{24,12},{28,16},{0,20},{4,24},{8,28},{13,1},{... | collective-permute-start | bytes 3145736 | tf_op jit(solution)/shard_map/ppermute | solution.py:12
  26.4 28.4 %collective-permute-start.2 = (f32[256,1024]{1,0:T(8,128)S(1)}, f32[256,1024]{1,0:T(8,128)S(1)}, u32[]{:S(2)}, u32[]{:S(2)}) collective-permute-start(f32[256,1024]{1,0:T(8,128)S(1)} %collective-permute-done), channel_id=1, source_target_pairs={{28,0},{0,4},{4,8},{8,12},{12,16},{16,20},{20,24},{24,28},{29,1},{... | collective-permute-start | bytes 3145736 | tf_op jit(solution)/shard_map/ppermute | solution.py:12
  54.8 16.0 %collective-permute-start.4 = (f32[256,1024]{1,0:T(8,128)S(1)}, f32[256,1024]{1,0:T(8,128)S(1)}, u32[]{:S(2)}, u32[]{:S(2)}) collective-permute-start(f32[256,1024]{1,0:T(8,128)S(1)} %collective-permute-done.2), channel_id=1, source_target_pairs={{28,0},{0,4},{4,8},{8,12},{12,16},{16,20},{20,24},{24,28},{29,1},{... | collective-permute-start | bytes 3145736 | tf_op jit(solution)/shard_map/ppermute | solution.py:12
  60.1 44.0 %copy-start.3 = (f32[1024]{0:T(1024)S(1)}, f32[1024]{0:T(1024)}, u32[]{:S(2)}) copy-start(f32[1024]{0:T(1024)} %param.13) | copy-start | bytes 12292
  60.1 44.0 %copy-start.6 = (s32[256]{0:T(256)S(1)}, s32[256]{0:T(256)}, u32[]{:S(2)}) copy-start(s32[256]{0:T(256)} %param.10) | copy-start | bytes 3076
  60.1 75.2 %copy-start.4 = (f32[256]{0:T(256)S(1)}, f32[256]{0:T(256)}, u32[]{:S(2)}) copy-start(f32[256]{0:T(256)} %param.12) | copy-start | bytes 3076
  60.1 75.2 %copy-start.5 = (s32[4,2]{0,1:T(2,128)S(1)}, s32[4,2]{0,1:T(2,128)}, u32[]{:S(2)}) copy-start(s32[4,2]{0,1:T(2,128)} %param.11) | copy-start | bytes 100
  60.1 75.5 %all-to-all-start = ((f32[4,256,1024]{1,0,2:T(4,128)}), f32[4,256,1024]{1,0,2:T(4,128)}, u32[]{:S(2)}, u32[]{:S(2)}) async-start(f32[4,256,1024]{1,0,2:T(4,128)} %copy.15), calls=%async_computation | async-start | bytes 8388608 | tf_op jit(solution)/shard_map/all_to_all | solution.py:39
  70.8 16.0 %collective-permute-start.6 = (f32[256,1024]{1,0:T(8,128)S(1)}, f32[256,1024]{1,0:T(8,128)S(1)}, u32[]{:S(2)}, u32[]{:S(2)}) collective-permute-start(f32[256,1024]{1,0:T(8,128)S(1)} %collective-permute-done.4), channel_id=1, source_target_pairs={{28,0},{0,4},{4,8},{8,12},{12,16},{16,20},{20,24},{24,28},{29,1},{... | collective-permute-start | bytes 3145736 | tf_op jit(solution)/shard_map/ppermute | solution.py:12
  86.8 1.1 copy-start.1
  87.9 16.1 %collective-permute-start.8 = (f32[256,1024]{1,0:T(8,128)S(1)}, f32[256,1024]{1,0:T(8,128)}, u32[]{:S(2)}, u32[]{:S(2)}) collective-permute-start(f32[256,1024]{1,0:T(8,128)S(1)} %collective-permute-done.6), channel_id=1, source_target_pairs={{28,0},{0,4},{4,8},{8,12},{12,16},{16,20},{20,24},{24,28},{29,1},{... | collective-permute-start | bytes 3145736 | tf_op jit(solution)/shard_map/ppermute | solution.py:12
  104.0 36.8 %collective-permute-start.10 = (f32[256,1024]{1,0:T(8,128)}, f32[256,1024]{1,0:T(8,128)}, u32[]{:S(2)}, u32[]{:S(2)}) collective-permute-start(f32[256,1024]{1,0:T(8,128)} %collective-permute-done.8), channel_id=1, source_target_pairs={{28,0},{0,4},{4,8},{8,12},{12,16},{16,20},{20,24},{24,28},{29,1},{... | collective-permute-start | bytes 3145736 | tf_op jit(solution)/shard_map/ppermute | solution.py:12
  104.3 3.1 collective-permute-start.1
  107.4 13.5 %collective-permute-start.3 = (f32[256]{0:T(256)S(1)}, f32[256]{0:T(256)S(1)}, u32[]{:S(2)}, u32[]{:S(2)}) collective-permute-start(f32[256]{0:T(256)S(1)} %collective-permute-done.1), channel_id=1, source_target_pairs={{28,0},{0,4},{4,8},{8,12},{12,16},{16,20},{20,24},{24,28},{29,1},{... | collective-permute-start | bytes 3080 | tf_op jit(solution)/shard_map/ppermute | solution.py:12
  120.9 4.8 %collective-permute-start.5 = (f32[256]{0:T(256)S(1)}, f32[256]{0:T(256)S(1)}, u32[]{:S(2)}, u32[]{:S(2)}) collective-permute-start(f32[256]{0:T(256)S(1)} %collective-permute-done.3), channel_id=1, source_target_pairs={{28,0},{0,4},{4,8},{8,12},{12,16},{16,20},{20,24},{24,28},{29,1},{... | collective-permute-start | bytes 3080 | tf_op jit(solution)/shard_map/ppermute | solution.py:12
  125.7 4.8 %collective-permute-start.7 = (f32[256]{0:T(256)S(1)}, f32[256]{0:T(256)S(1)}, u32[]{:S(2)}, u32[]{:S(2)}) collective-permute-start(f32[256]{0:T(256)S(1)} %collective-permute-done.5), channel_id=1, source_target_pairs={{28,0},{0,4},{4,8},{8,12},{12,16},{16,20},{20,24},{24,28},{29,1},{... | collective-permute-start | bytes 3080 | tf_op jit(solution)/shard_map/ppermute | solution.py:12
  130.5 4.8 %collective-permute-start.9 = (f32[256]{0:T(256)S(1)}, f32[256]{0:T(256)S(1)}, u32[]{:S(2)}, u32[]{:S(2)}) collective-permute-start(f32[256]{0:T(256)S(1)} %collective-permute-done.7), channel_id=1, source_target_pairs={{28,0},{0,4},{4,8},{8,12},{12,16},{16,20},{20,24},{24,28},{29,1},{... | collective-permute-start | bytes 3080 | tf_op jit(solution)/shard_map/ppermute | solution.py:12
  135.3 5.5 %collective-permute-start.11 = (f32[256]{0:T(256)S(1)}, f32[256]{0:T(256)S(1)}, u32[]{:S(2)}, u32[]{:S(2)}) collective-permute-start(f32[256]{0:T(256)S(1)} %collective-permute-done.9), channel_id=1, source_target_pairs={{28,0},{0,4},{4,8},{8,12},{12,16},{16,20},{20,24},{24,28},{29,1},{... | collective-permute-start | bytes 3080 | tf_op jit(solution)/shard_map/ppermute | solution.py:12
  141.0 5.8 %copy-start = (f32[4,1024,256]{2,1,0:T(8,128)S(1)}, f32[4,1024,256]{2,1,0:T(8,128)}, u32[]{:S(2)}) copy-start(f32[4,1024,256]{2,1,0:T(8,128)} %get-tuple-element.270) | copy-start | bytes 12582916 | tf_op jit(solution)/shard_map/while
  149.3 4.6 %copy-start.2 = (f32[256,1024]{1,0:T(8,128)S(1)}, f32[256,1024]{1,0:T(8,128)}, u32[]{:S(2)}) copy-start(f32[256,1024]{1,0:T(8,128)} %get-tuple-element.279) | copy-start | bytes 3145732 | tf_op jit(solution)/shard_map/while
  197.4 5.8 %copy-start = (f32[4,1024,256]{2,1,0:T(8,128)S(1)}, f32[4,1024,256]{2,1,0:T(8,128)}, u32[]{:S(2)}) copy-start(f32[4,1024,256]{2,1,0:T(8,128)} %get-tuple-element.270) | copy-start | bytes 12582916 | tf_op jit(solution)/shard_map/while
  205.7 4.6 %copy-start.2 = (f32[256,1024]{1,0:T(8,128)S(1)}, f32[256,1024]{1,0:T(8,128)}, u32[]{:S(2)}) copy-start(f32[256,1024]{1,0:T(8,128)} %get-tuple-element.279) | copy-start | bytes 3145732 | tf_op jit(solution)/shard_map/while
  253.7 5.8 %copy-start = (f32[4,1024,256]{2,1,0:T(8,128)S(1)}, f32[4,1024,256]{2,1,0:T(8,128)}, u32[]{:S(2)}) copy-start(f32[4,1024,256]{2,1,0:T(8,128)} %get-tuple-element.270) | copy-start | bytes 12582916 | tf_op jit(solution)/shard_map/while
  262.0 4.6 %copy-start.2 = (f32[256,1024]{1,0:T(8,128)S(1)}, f32[256,1024]{1,0:T(8,128)}, u32[]{:S(2)}) copy-start(f32[256,1024]{1,0:T(8,128)} %get-tuple-element.279) | copy-start | bytes 3145732 | tf_op jit(solution)/shard_map/while
  310.1 5.8 %copy-start = (f32[4,1024,256]{2,1,0:T(8,128)S(1)}, f32[4,1024,256]{2,1,0:T(8,128)}, u32[]{:S(2)}) copy-start(f32[4,1024,256]{2,1,0:T(8,128)} %get-tuple-element.270) | copy-start | bytes 12582916 | tf_op jit(solution)/shard_map/while
  318.4 4.6 %copy-start.2 = (f32[256,1024]{1,0:T(8,128)S(1)}, f32[256,1024]{1,0:T(8,128)}, u32[]{:S(2)}) copy-start(f32[256,1024]{1,0:T(8,128)} %get-tuple-element.279) | copy-start | bytes 3145732 | tf_op jit(solution)/shard_map/while
where the time goes:
time: 429 us; the launch traced here: 425 us
  local copies, waits for them, and re-layouts  132 us (31%)
  matrix products  115 us (27%)
  waiting for transfers between devices  104 us (24%)
  blocking collectives  48.4 us (11%)
  starting transfers between devices  24.3 us (6%)
    dynamic_update_slice x8, local copies, waits for them, and re-layouts, local(): totals = lax.map(pair_columns, (factors, pair_energy))  107 us
    ppermute x12, waiting for transfers between devices, passed_along(): return lax.ppermute(block, axis, route)  104 us
    dot_general x24, matrix products, pair_columns(): jnp.dot(block, factor, precision=lax.Precision.HIGHEST, preferred_element...  76.2 us
    all_to_all x1, blocking collectives, local(): return lax.all_to_all(totals, 'vb', split_axis=1, concat_axis=2, tiled=True)  48.4 us
    dot_general x24, matrix products, pair_columns(): jnp.dot(block.T, weighted / denom, precision=lax.Precision.HIGHEST, prefe...  38.5 us
    ppermute x12, starting transfers between devices, passed_along(): return lax.ppermute(block, axis, route)  19.3 us
    all_to_all x2, local copies, waits for them, and re-layouts, local(): return lax.all_to_all(totals, 'vb', split_axis=1, concat_axis=2, tiled=True)  10.4 us
  transfers between devices with their start and end apart: 13, of which 10 were waited for; matrix products, arithmetic and copies ran while one was open for 3% of the time, Pallas kernels for 0%

commit v1 on v0

--- a/solution.py
+++ b/solution.py
@@ -4,6 +4,28 @@
 from jax.sharding import PartitionSpec as P
 
 HOPS = 5
+
+
+def in_blocks(x, dim, length):
+    before, after = (x.shape[:dim], x.shape[dim + 1 :])
+    return jnp.moveaxis(x.reshape(*before, length, -1, *after), dim, 0)
+
+
+def in_order(tiles, dim):
+    tiles = jnp.moveaxis(tiles, 0, dim)
+    dims = tiles.shape
+    return tiles.reshape(*dims[:dim], dims[dim] * dims[dim + 1], *dims[dim + 2 :])
+
+
+def exchange_in_pairs(array, axis, split_dim, concat_dim):
+    size, index = (lax.axis_size(axis), lax.axis_index(axis))
+    blocks = in_blocks(array, split_dim, size)
+    outs = [blocks[index]]
+    for turn in range(1, size):
+        sent = blocks[index ^ turn]
+        outs.append(lax.ppermute(sent, axis, [(i, i ^ turn) for i in range(size)]))
+    blocks = jnp.stack(outs)[index ^ jnp.arange(size)]
+    return in_order(blocks, concat_dim)
 
 
 def passed_along(block, axis, distance):
@@ -36,7 +58,7 @@
     for turn in range(HOPS):
         current = step_down(current)
         window.append(current)
-    factors = lax.all_to_all(amplitudes, "vb", split_axis=2, concat_axis=1, tiled=True)
+    factors = exchange_in_pairs(amplitudes, "vb", 2, 1)
 
     def pair_columns(inputs):
         factor, energy = inputs

time: 429 us -> 461 us (1.075)
  local copies, waits for them, and re-layouts: 132 us -> 153 us
  matrix products: 115 us -> 123 us
    another operation x0 -> x1, local copies, waits for them, and re-layouts: none -> 11.5 us
    ppermute x12, waiting for transfers between devices: 104 us -> 94.2 us  [passed_along(): return lax.ppermute(block, axis, route)]
    ppermute x0 -> x3, waiting for transfers between devices: none -> 9.3 us  [exchange_in_pairs(): outs.append(lax.ppermute(sent, axis, [(i, i ^ turn) for i in range(size)]))]
    reshape x0 -> x1, local copies, waits for them, and re-layouts: none -> 5.61 us  [in_blocks(): return jnp.moveaxis(x.reshape(*before, length, -1, *after), dim, 0)]
    all_to_all x1 -> x0, local copies, waits for them, and re-layouts: 5.25 us -> none  [local(): lax.all_to_all(amplitudes, 'vb', split_axis=2, concat_axis=1, tiled=True)]
    all_to_all x1 -> x0, starting transfers between devices: 5 us -> none  [local(): lax.all_to_all(amplitudes, 'vb', split_axis=2, concat_axis=1, tiled=True)]
    gather x0 -> x1, local copies, waits for them, and re-layouts: none -> 4.98 us  [exchange_in_pairs(): blocks = jnp.stack(outs)[index ^ jnp.arange(size)]]
    dot_general x24, matrix products: 38.5 us -> 43.4 us  [pair_columns(): jnp.dot(block.T, weighted / denom, precision=lax.Precision.HIGHEST, prefe...]
  transfers between devices with their start and end apart: 13 -> 15, of which waited for: 10 -> 10; matrix products, arithmetic and copies ran while one was open for 3% -> 8% of each run, Pallas kernels for 0% -> 0%
where the time goes in v1:
time: 461 us; the launch traced here: 455 us
  local copies, waits for them, and re-layouts  153 us (33%)
  matrix products  123 us (27%)
  waiting for transfers between devices  103 us (22%)
  blocking collectives  45.9 us (10%)
  starting transfers between devices  24.6 us (5%)
  other arithmetic  4.98 us (1%)
    dynamic_update_slice x8, local copies, waits for them, and re-layouts, local(): totals = lax.map(pair_columns, (factors, pair_energy))  107 us
    ppermute x12, waiting for transfers between devices, passed_along(): return lax.ppermute(block, axis, route)  94.2 us
    dot_general x24, matrix products, pair_columns(): jnp.dot(block, factor, precision=lax.Precision.HIGHEST, preferred_element...  79.6 us
    all_to_all x1, blocking collectives, local(): return lax.all_to_all(totals, 'vb', split_axis=1, concat_axis=2, tiled=True)  45.9 us
    dot_general x24, matrix products, pair_columns(): jnp.dot(block.T, weighted / denom, precision=lax.Precision.HIGHEST, prefe...  43.4 us
    ppermute x12, starting transfers between devices, passed_along(): return lax.ppermute(block, axis, route)  21.2 us
    another operation x1, local copies, waits for them, and re-layouts  11.5 us
    all_to_all x2, local copies, waits for them, and re-layouts, local(): return lax.all_to_all(totals, 'vb', split_axis=1, concat_axis=2, tiled=True)  10.4 us
  transfers between devices with their start and end apart: 15, of which 10 were waited for; matrix products, arithmetic and copies ran while one was open for 8% of the time, Pallas kernels for 0%

profile of v1, /device:TPU:0, one launch (start us, length us, event | category | flops | bytes accessed | tf_op | source)
XLA Modules:
  0.0 455.1 jit_solution(4471318071650318851)
XLA Ops:
  3.5 22.9 %collective-permute-done.3 = f32[256,1024]{1,0:T(8,128)S(1)} collective-permute-done((f32[256,1024]{1,0:T(8,128)}, f32[256,1024]{1,0:T(8,128)S(1)}, u32[]{:S(2)}, u32[]{:S(2)}) %collective-permute-start.3) | collective-permute-done | bytes 1048608 | tf_op jit(solution)/shard_map/ppermute | solution.py:34
  26.4 12.8 %collective-permute-start.5 = (f32[256,1024]{1,0:T(8,128)S(1)}, f32[256,1024]{1,0:T(8,128)S(1)}, u32[]{:S(2)}, u32[]{:S(2)}) collective-permute-start(f32[256,1024]{1,0:T(8,128)S(1)} %collective-permute-done.3), channel_id=1, source_target_pairs={{28,0},{0,4},{4,8},{8,12},{12,16},{16,20},{20,24},{24,28},{29,1},{... | collective-permute-start | bytes 3145736 | tf_op jit(solution)/shard_map/ppermute | solution.py:34
  39.2 15.6 %collective-permute-done.5 = f32[256,1024]{1,0:T(8,128)S(1)} collective-permute-done((f32[256,1024]{1,0:T(8,128)S(1)}, f32[256,1024]{1,0:T(8,128)S(1)}, u32[]{:S(2)}, u32[]{:S(2)}) %collective-permute-start.5) | collective-permute-done | bytes 1048608 | tf_op jit(solution)/shard_map/ppermute | solution.py:34
  54.8 16.0 %collective-permute-done.7 = f32[256,1024]{1,0:T(8,128)S(1)} collective-permute-done((f32[256,1024]{1,0:T(8,128)S(1)}, f32[256,1024]{1,0:T(8,128)S(1)}, u32[]{:S(2)}, u32[]{:S(2)}) %collective-permute-start.7) | collective-permute-done | bytes 1048608 | tf_op jit(solution)/shard_map/ppermute | solution.py:34
  70.8 16.1 %collective-permute-done.9 = f32[256,1024]{1,0:T(8,128)} collective-permute-done((f32[256,1024]{1,0:T(8,128)S(1)}, f32[256,1024]{1,0:T(8,128)}, u32[]{:S(2)}, u32[]{:S(2)}) %collective-permute-start.9) | collective-permute-done | bytes 1048608 | tf_op jit(solution)/shard_map/ppermute | solution.py:34
  86.9 5.6 %reshape.40 = f32[4,256,4,256]{3,2,1,0:T(4,128)} reshape(f32[4,256,1024]{2,1,0:T(8,128)} %param.8) | data formatting | bytes 8388608 | tf_op jit(solution)/shard_map/reshape | solution.py:11
  92.6 11.5 %constant_dynamic-slice_fusion.3 = (f32[4,256,1,256]{3,2,1,0:T(1,128)}, f32[4,256,1,256]{3,2,1,0:T(1,128)S(1)}, f32[4,256,1,256]{3,2,1,0:T(1,128)S(1)}, f32[4,256,1,256]{3,2,1,0:T(1,128)S(1)}) fusion(f32[4,256,4,256]{3,2,1,0:T(4,128)} %reshape.40, s32[]{:T(128)S(6)} %select_n.33, s32[]{:T(128)S(6)} %select_n.35, s32[]{:T(128)S(6)} %select_n.34, s32[]{:T(128)S(6)} %select_n.36), kind=kLoop, calls=%fused_computation.51 | loop fusion | bytes 8388624 | tf_op jit(solution)/shard_map/dynamic-slice
  114.0 4.8 %collective-permute-start.6 = (f32[256]{0:T(256)S(1)}, f32[256]{0:T(256)S(1)}, u32[]{:S(2)}, u32[]{:S(2)}) collective-permute-start(f32[256]{0:T(256)S(1)} %collective-permute-done.4), channel_id=1, source_target_pairs={{28,0},{0,4},{4,8},{8,12},{12,16},{16,20},{20,24},{24,28},{29,1},{... | collective-permute-start | bytes 3080 | tf_op jit(solution)/shard_map/ppermute | solution.py:34
  118.8 8.8 %collective-permute-done.6 = f32[256]{0:T(256)S(1)} collective-permute-done((f32[256]{0:T(256)S(1)}, f32[256]{0:T(256)S(1)}, u32[]{:S(2)}, u32[]{:S(2)}) %collective-permute-start.6) | collective-permute-done | bytes 1056 | tf_op jit(solution)/shard_map/ppermute | solution.py:34
  127.8 4.6 %collective-permute-done.8 = f32[256]{0:T(256)S(1)} collective-permute-done((f32[256]{0:T(256)S(1)}, f32[256]{0:T(256)S(1)}, u32[]{:S(2)}, u32[]{:S(2)}) %collective-permute-start.8) | collective-permute-done | bytes 1056 | tf_op jit(solution)/shard_map/ppermute | solution.py:34
  132.4 4.8 %collective-permute-done.10 = f32[256]{0:T(256)S(1)} collective-permute-done((f32[256]{0:T(256)S(1)}, f32[256]{0:T(256)S(1)}, u32[]{:S(2)}, u32[]{:S(2)}) %collective-permute-start.10) | collective-permute-done | bytes 1056 | tf_op jit(solution)/shard_map/ppermute | solution.py:34
  142.0 9.3 %collective-permute-done.1 = f32[4,256,256]{2,1,0:T(8,128)} collective-permute-done((f32[4,256,256]{2,1,0:T(8,128)}, f32[4,256,256]{2,1,0:T(8,128)}, u32[]{:S(2)}, u32[]{:S(2)}) %collective-permute-start.1) | collective-permute-done | bytes 1048608 | tf_op jit(solution)/shard_map/ppermute | solution.py:26
  151.3 4.5 pad_maximum_fusion
  155.8 5.0 %gather_fusion = f32[4,4,256,256]{3,2,1,0:T(8,128)} fusion(f32[4,4,256,256]{3,2,1,0:T(8,128)} %pad_maximum_fusion, s32[1024]{0:T(1024)S(1)} %pad_clamp_fusion), kind=kCustom, calls=%fused_computation | custom fusion | bytes 8388624 | tf_op jit(solution)/shard_map/gather | solution.py:27
  160.8 4.6 %copy.34 = f32[4,4,256,256]{3,2,1,0:T(8,128)} copy(f32[4,4,256,256]{3,2,0,1:T(8,128)} %bitcast.147) | data formatting | bytes 8388608 | tf_op jit(solution)/shard_map/transpose | solution.py:15
  165.4 233.3 %while.10 = (s32[]{:T(128)}, f32[4,1024,256]{2,0,1:T(4,128)}, f32[4,1024,256]{2,1,0:T(8,128)}, f32[256,1024]{1,0:T(8,128)S(1)}, f32[256]{0:T(256)S(1)}, /*index=...) while((s32[]{:T(128)}, f32[4,1024,256]{2,0,1:T(4,128)}, ...), condition=%wide.region_3.4_spmd, body=%wide.region_2.3_spmd.sunk | while | flops 9666166784 | bytes 54539520 | solution.py:79
  166.0 4.0 fusion.101
  178.0 3.7 fusion.105
  183.9 3.7 fusion.106
  200.4 23.2 %dynamic_update_slice.5 = f32[4,1024,256]{2,0,1:T(4,128)} dynamic-update-slice(f32[4,1024,256]{2,0,1:T(4,128)} %get-tuple-element.254, f32[1,1024,256]{2,0,1:T(1,128)} %copy.54, s32[]{:T(128)} %get-tuple-element.253, s32[]{:T(128)} %constant.3.clone.1..sunk, s32[]{:T(128)} %constant.3.clone.1..sunk) | dynamic-update-slice | bytes 2097156 | tf_op jit(solution)/shard_map/while/body/jit(dynamic_update_index_in_dim)/dynamic_update_slice | solution.py:79
  224.3 4.0 fusion.101
  242.3 3.7 fusion.106
  258.8 23.2 %dynamic_update_slice.5 = f32[4,1024,256]{2,0,1:T(4,128)} dynamic-update-slice(f32[4,1024,256]{2,0,1:T(4,128)} %get-tuple-element.254, f32[1,1024,256]{2,0,1:T(1,128)} %copy.54, s32[]{:T(128)} %get-tuple-element.253, s32[]{:T(128)} %constant.3.clone.1..sunk, s32[]{:T(128)} %constant.3.clone.1..sunk) | dynamic-update-slice | bytes 2097156 | tf_op jit(solution)/shard_map/while/body/jit(dynamic_update_index_in_dim)/dynamic_update_slice | solution.py:79
  282.6 4.0 fusion.101
  300.6 3.7 fusion.106
  317.1 23.2 %dynamic_update_slice.5 = f32[4,1024,256]{2,0,1:T(4,128)} dynamic-update-slice(f32[4,1024,256]{2,0,1:T(4,128)} %get-tuple-element.254, f32[1,1024,256]{2,0,1:T(1,128)} %copy.54, s32[]{:T(128)} %get-tuple-element.253, s32[]{:T(128)} %constant.3.clone.1..sunk, s32[]{:T(128)} %constant.3.clone.1..sunk) | dynamic-update-slice | bytes 2097156 | tf_op jit(solution)/shard_map/while/body/jit(dynamic_update_index_in_dim)/dynamic_update_slice | solution.py:79
  341.0 4.0 fusion.101
  358.9 3.7 fusion.106
  375.4 23.2 %dynamic_update_slice.5 = f32[4,1024,256]{2,0,1:T(4,128)} dynamic-update-slice(f32[4,1024,256]{2,0,1:T(4,128)} %get-tuple-element.254, f32[1,1024,256]{2,0,1:T(1,128)} %copy.54, s32[]{:T(128)} %get-tuple-element.253, s32[]{:T(128)} %constant.3.clone.1..sunk, s32[]{:T(128)} %constant.3.clone.1..sunk) | dynamic-update-slice | bytes 2097156 | tf_op jit(solution)/shard_map/while/body/jit(dynamic_update_index_in_dim)/dynamic_update_slice | solution.py:79
  398.7 45.9 %all_to_all.18 = f32[4,1024,256]{2,0,1:T(4,128)S(1)} all-to-all(f32[4,1024,256]{2,0,1:T(4,128)} %get-tuple-element.92), channel_id=1, replica_groups=mesh['blk'=8,'vb'=4] {'vb'}, dimensions={1} | all-to-all | bytes 8388608 | tf_op jit(solution)/shard_map/all_to_all | solution.py:80
  444.6 4.7 %copy.36 = f32[4,256,4,256]{3,2,1,0:T(4,128)} copy(f32[4,256,4,256]{3,0,1,2:T(4,128)S(1)} %bitcast.148) | data formatting | bytes 8388608 | tf_op jit(solution)/shard_map/all_to_all | solution.py:80
  449.3 5.8 %all_to_all.16 = f32[4,256,1024]{2,1,0:T(8,128)} reshape(f32[4,256,4,256]{3,2,1,0:T(4,128)} %copy.36) | data formatting | bytes 8388608 | tf_op jit(solution)/shard_map/all_to_all | solution.py:80
  (93 shorter events, 124.1 us)
Async XLA Ops:
  0.0 26.4 %collective-permute-start.3 = (f32[256,1024]{1,0:T(8,128)}, f32[256,1024]{1,0:T(8,128)S(1)}, u32[]{:S(2)}, u32[]{:S(2)}) collective-permute-start(f32[256,1024]{1,0:T(8,128)} %param.9), channel_id=1, source_target_pairs={{12,0},{16,4},{20,8},{24,12},{28,16},{0,20},{4,24},{8,28},{13,1},{... | collective-permute-start | bytes 3145736 | tf_op jit(solution)/shard_map/ppermute | solution.py:34
  26.4 28.4 %collective-permute-start.5 = (f32[256,1024]{1,0:T(8,128)S(1)}, f32[256,1024]{1,0:T(8,128)S(1)}, u32[]{:S(2)}, u32[]{:S(2)}) collective-permute-start(f32[256,1024]{1,0:T(8,128)S(1)} %collective-permute-done.3), channel_id=1, source_target_pairs={{28,0},{0,4},{4,8},{8,12},{12,16},{16,20},{20,24},{24,28},{29,1},{... | collective-permute-start | bytes 3145736 | tf_op jit(solution)/shard_map/ppermute | solution.py:34
  54.8 16.0 %collective-permute-start.7 = (f32[256,1024]{1,0:T(8,128)S(1)}, f32[256,1024]{1,0:T(8,128)S(1)}, u32[]{:S(2)}, u32[]{:S(2)}) collective-permute-start(f32[256,1024]{1,0:T(8,128)S(1)} %collective-permute-done.5), channel_id=1, source_target_pairs={{28,0},{0,4},{4,8},{8,12},{12,16},{16,20},{20,24},{24,28},{29,1},{... | collective-permute-start | bytes 3145736 | tf_op jit(solution)/shard_map/ppermute | solution.py:34
  70.8 16.1 %collective-permute-start.9 = (f32[256,1024]{1,0:T(8,128)S(1)}, f32[256,1024]{1,0:T(8,128)}, u32[]{:S(2)}, u32[]{:S(2)}) collective-permute-start(f32[256,1024]{1,0:T(8,128)S(1)} %collective-permute-done.7), channel_id=1, source_target_pairs={{28,0},{0,4},{4,8},{8,12},{12,16},{16,20},{20,24},{24,28},{29,1},{... | collective-permute-start | bytes 3145736 | tf_op jit(solution)/shard_map/ppermute | solution.py:34
  86.9 23.8 %collective-permute-start.11 = (f32[256,1024]{1,0:T(8,128)}, f32[256,1024]{1,0:T(8,128)}, u32[]{:S(2)}, u32[]{:S(2)}) collective-permute-start(f32[256,1024]{1,0:T(8,128)} %collective-permute-done.9), channel_id=1, source_target_pairs={{28,0},{0,4},{4,8},{8,12},{12,16},{16,20},{20,24},{24,28},{29,1},{... | collective-permute-start | bytes 3145736 | tf_op jit(solution)/shard_map/ppermute | solution.py:34
  104.1 6.6 %copy-start.1 = (f32[1024]{0:T(1024)S(1)}, f32[1024]{0:T(1024)}, u32[]{:S(2)}) copy-start(f32[1024]{0:T(1024)} %param.13) | copy-start | bytes 12292
  104.1 6.7 %copy-start.4 = (s32[256]{0:T(256)S(1)}, s32[256]{0:T(256)}, u32[]{:S(2)}) copy-start(s32[256]{0:T(256)} %param.10) | copy-start | bytes 3076
  104.1 23.5 %copy-start.2 = (f32[256]{0:T(256)S(1)}, f32[256]{0:T(256)}, u32[]{:S(2)}) copy-start(f32[256]{0:T(256)} %param.12) | copy-start | bytes 3076
  104.1 23.5 %copy-start.3 = (s32[4,2]{0,1:T(2,128)S(1)}, s32[4,2]{0,1:T(2,128)}, u32[]{:S(2)}) copy-start(s32[4,2]{0,1:T(2,128)} %param.11) | copy-start | bytes 100
  105.1 36.8 %collective-permute-start = (f32[4,256,256]{2,1,0:T(8,128)}, f32[4,256,256]{2,1,0:T(8,128)}, u32[]{:S(2)}, u32[]{:S(2)}) collective-permute-start(f32[4,256,256]{2,1,0:T(8,128)} %bitcast.80), channel_id=1, source_target_pairs={{0,1},{1,0},{2,3},{3,2},{4,5},{5,4},{6,7},{7,6},{8,9},{9,8},{10,11... | collective-permute-start | bytes 3145736 | tf_op jit(solution)/shard_map/ppermute | solution.py:26
  107.7 43.6 %collective-permute-start.1 = (f32[4,256,256]{2,1,0:T(8,128)}, f32[4,256,256]{2,1,0:T(8,128)}, u32[]{:S(2)}, u32[]{:S(2)}) collective-permute-start(f32[4,256,256]{2,1,0:T(8,128)} %bitcast.79), channel_id=1, source_target_pairs={{0,2},{1,3},{2,0},{3,1},{4,6},{5,7},{6,4},{7,5},{8,10},{9,11},{10,... | collective-permute-start | bytes 3145736 | tf_op jit(solution)/shard_map/ppermute | solution.py:26
  110.2 41.0 %collective-permute-start.2 = (f32[4,256,256]{2,1,0:T(8,128)}, f32[4,256,256]{2,1,0:T(8,128)}, u32[]{:S(2)}, u32[]{:S(2)}) collective-permute-start(f32[4,256,256]{2,1,0:T(8,128)} %bitcast.78), channel_id=1, source_target_pairs={{0,3},{1,2},{2,1},{3,0},{4,7},{5,6},{6,5},{7,4},{8,11},{9,10},{10,... | collective-permute-start | bytes 3145736 | tf_op jit(solution)/shard_map/ppermute | solution.py:26
  110.7 54.6 %collective-permute-start.13 = (f32[256,1024]{1,0:T(8,128)}, f32[256,1024]{1,0:T(8,128)}, u32[]{:S(2)}, u32[]{:S(2)}) collective-permute-start(f32[256,1024]{1,0:T(8,128)} %collective-permute-done.11), channel_id=1, source_target_pairs={{28,0},{0,4},{4,8},{8,12},{12,16},{16,20},{20,24},{24,28},{29,1},{... | collective-permute-start | bytes 3145736 | tf_op jit(solution)/shard_map/ppermute | solution.py:34
  111.0 3.1 collective-permute-start.4
  114.0 13.5 %collective-permute-start.6 = (f32[256]{0:T(256)S(1)}, f32[256]{0:T(256)S(1)}, u32[]{:S(2)}, u32[]{:S(2)}) collective-permute-start(f32[256]{0:T(256)S(1)} %collective-permute-done.4), channel_id=1, source_target_pairs={{28,0},{0,4},{4,8},{8,12},{12,16},{16,20},{20,24},{24,28},{29,1},{... | collective-permute-start | bytes 3080 | tf_op jit(solution)/shard_map/ppermute | solution.py:34
  127.6 4.8 %collective-permute-start.8 = (f32[256]{0:T(256)S(1)}, f32[256]{0:T(256)S(1)}, u32[]{:S(2)}, u32[]{:S(2)}) collective-permute-start(f32[256]{0:T(256)S(1)} %collective-permute-done.6), channel_id=1, source_target_pairs={{28,0},{0,4},{4,8},{8,12},{12,16},{16,20},{20,24},{24,28},{29,1},{... | collective-permute-start | bytes 3080 | tf_op jit(solution)/shard_map/ppermute | solution.py:34
  132.4 4.8 %collective-permute-start.10 = (f32[256]{0:T(256)S(1)}, f32[256]{0:T(256)S(1)}, u32[]{:S(2)}, u32[]{:S(2)}) collective-permute-start(f32[256]{0:T(256)S(1)} %collective-permute-done.8), channel_id=1, source_target_pairs={{28,0},{0,4},{4,8},{8,12},{12,16},{16,20},{20,24},{24,28},{29,1},{... | collective-permute-start | bytes 3080 | tf_op jit(solution)/shard_map/ppermute | solution.py:34
  137.2 4.8 %collective-permute-start.12 = (f32[256]{0:T(256)S(1)}, f32[256]{0:T(256)S(1)}, u32[]{:S(2)}, u32[]{:S(2)}) collective-permute-start(f32[256]{0:T(256)S(1)} %collective-permute-done.10), channel_id=1, source_target_pairs={{28,0},{0,4},{4,8},{8,12},{12,16},{16,20},{20,24},{24,28},{29,1},{... | collective-permute-start | bytes 3080 | tf_op jit(solution)/shard_map/ppermute | solution.py:34
  142.0 23.4 %collective-permute-start.14 = (f32[256]{0:T(256)S(1)}, f32[256]{0:T(256)S(1)}, u32[]{:S(2)}, u32[]{:S(2)}) collective-permute-start(f32[256]{0:T(256)S(1)} %collective-permute-done.12), channel_id=1, source_target_pairs={{28,0},{0,4},{4,8},{8,12},{12,16},{16,20},{20,24},{24,28},{29,1},{... | collective-permute-start | bytes 3080 | tf_op jit(solution)/shard_map/ppermute | solution.py:34
  165.4 5.6 %copy-start = (f32[4,1024,256]{2,1,0:T(8,128)S(1)}, f32[4,1024,256]{2,1,0:T(8,128)}, u32[]{:S(2)}) copy-start(f32[4,1024,256]{2,1,0:T(8,128)} %get-tuple-element.274) | copy-start | bytes 12582916 | tf_op jit(solution)/shard_map/while
  223.7 5.6 %copy-start = (f32[4,1024,256]{2,1,0:T(8,128)S(1)}, f32[4,1024,256]{2,1,0:T(8,128)}, u32[]{:S(2)}) copy-start(f32[4,1024,256]{2,1,0:T(8,128)} %get-tuple-element.274) | copy-start | bytes 12582916 | tf_op jit(solution)/shard_map/while
  282.0 5.6 %copy-start = (f32[4,1024,256]{2,1,0:T(8,128)S(1)}, f32[4,1024,256]{2,1,0:T(8,128)}, u32[]{:S(2)}) copy-start(f32[4,1024,256]{2,1,0:T(8,128)} %get-tuple-element.274) | copy-start | bytes 12582916 | tf_op jit(solution)/shard_map/while
  340.3 5.6 %copy-start = (f32[4,1024,256]{2,1,0:T(8,128)S(1)}, f32[4,1024,256]{2,1,0:T(8,128)}, u32[]{:S(2)}) copy-start(f32[4,1024,256]{2,1,0:T(8,128)} %get-tuple-element.274) | copy-start | bytes 12582916 | tf_op jit(solution)/shard_map/while
